TPU v7x, 32 devices: a whole 2x2x4 slice. The times are simulated.
32 devices in a mesh: batch: 8 (over z, x), phase: 2 (over core), mp: 2 (over y).
Axes of the slice: x: 2, y: 2, z: 4, core: 2. Of those that a mesh axis runs over, the one named last changes fastest.
Arguments:
- images: bfloat16 [64, 4, 4, 768], P('batch'), may hold values from -6 to 6
- conv_kernels: float32 [2, 7, 7, 768], P('phase'), may hold values from -0.875 to 0.875
- norm_gains: float32 [2, 768], P('phase'), may hold values from 0.1 to 1.9
- expand_weight: bfloat16 [2, 768, 3072], P('phase', None, 'mp'), may hold values from -0.21875 to 0.21875
- project_weight: bfloat16 [2, 3072, 768], P('phase', 'mp'), may hold values from -0.109375 to 0.109375
- head_weight: bfloat16 [768, 1024], replicated, may hold values from -0.21875 to 0.21875
- texts: bfloat16 [64, 1024], P('batch'), may hold values from -6 to 6
- pair_index: int32 [64], P('batch'), may hold values from 0 to 63
Outputs:
- input_grads: float32 [2, 64, 4, 4, 768], P('phase', 'batch')
Inputs may be any that keep to these rules, and one draw needn't show every extreme that they name: Image i and text pair_index[i] form a positive pair.
All inputs are finite; a program needn't handle non-finite values.
Results may differ from a plain program's by a relative error of at most 0.018.
Values may be sent and summed in bfloat16 or wider, within the bound.
No kernel may reach another device: no remote copies, remote signals or barrier semaphores. Data moves between devices by JAX's collectives and lax.ppermute only.
A program may use at most 64 MiB of HBM per device.

v0:
```python
import jax
import jax.numpy as jnp
import numpy as np
from jax import lax
from jax.sharding import PartitionSpec as P

inverse_softness_factor = 30.0


def swapped(value, axis, stride):
    return lax.ppermute(value, axis, [(i, i ^ 1 << stride) for i in range(lax.axis_size(axis))])


def depthwise(values, kernel):
    kernel_side = kernel.shape[0]
    margin = kernel_side // 2
    grid_side = values.shape[1]
    cells = np.arange(grid_side * grid_side)
    cell_row = cells // grid_side
    cell_col = cells % grid_side
    tap_row = np.clip(cell_row[None, :] - cell_row[:, None] + margin, 0, kernel_side - 1)
    tap_col = np.clip(cell_col[None, :] - cell_col[:, None] + margin, 0, kernel_side - 1)
    inside = (
        (np.abs(cell_row[None, :] - cell_row[:, None]) <= margin)
        & (np.abs(cell_col[None, :] - cell_col[:, None]) <= margin)
    ).astype(np.float32)
    operator = kernel[tap_row, tap_col] * jnp.asarray(inside, dtype=kernel.dtype)[:, :, None]
    flat = values.reshape(values.shape[0], grid_side * grid_side, values.shape[3])
    result = jnp.einsum("oic,bic->boc", operator, flat, precision=lax.Precision.HIGHEST)
    return result.reshape(values.shape)


def normalize_last(values):
    centred = values - jnp.mean(values, axis=-1, keepdims=True)
    variance = jnp.mean(centred * centred, axis=-1, keepdims=True)
    return centred * lax.rsqrt(variance + 1e-06)


def front_part(values, kernel, gain_vec):
    return normalize_last(depthwise(values, kernel)) * gain_vec


def mlp_part(normed, expand, project_out):
    flattened = normed.reshape(-1, normed.shape[-1]).astype(jnp.bfloat16)
    hidden = jax.nn.gelu(jnp.dot(flattened, expand, preferred_element_type=jnp.float32)).astype(
        jnp.bfloat16
    )
    return jnp.dot(hidden, project_out, preferred_element_type=jnp.float32).reshape(normed.shape)


def head_part(values, head_weight):
    pooled = jnp.mean(values, axis=(1, 2))
    normed = normalize_last(pooled).astype(jnp.bfloat16)
    embedded = jnp.dot(normed, head_weight, preferred_element_type=jnp.float32)
    return embedded * lax.rsqrt(jnp.sum(embedded * embedded, axis=-1, keepdims=True) + 1e-06)


def unit_text(texts):
    widened = texts.astype(jnp.float32)
    return (widened * lax.rsqrt(jnp.sum(widened * widened, axis=-1, keepdims=True) + 1e-06)).astype(
        jnp.bfloat16
    )


def hidden_total(values):
    return lax.psum(values.astype(jnp.bfloat16), "mp").astype(jnp.float32)


def hand_over(values):
    return swapped(values, "phase", 0)


def section_forward(inputs_low, kernel, gain_vec, expand, project_out):
    widened = inputs_low.astype(jnp.float32)
    normed, front_back = jax.vjp(lambda inner: front_part(inner, kernel, gain_vec), widened)
    partial_out, mlp_back = jax.vjp(lambda inner: mlp_part(inner, expand, project_out), normed)
    summed = hidden_total(partial_out)
    return ((widened + summed).astype(jnp.bfloat16), front_back, mlp_back)


def section_backward(cotangent, front_back, mlp_back):
    (partial_grad,) = mlp_back(cotangent)
    (from_front,) = front_back(hidden_total(partial_grad))
    return cotangent + from_front


def make_fold(vector_lowered_total, pair_index, row_map):

    def fold_texts(state_now, text_block, first_row):
        block_rows = text_block.shape[0]
        cosine_score_matrix = inverse_softness_factor * jnp.einsum(
            "ie,je->ij", vector_lowered_total, text_block, preferred_element_type=jnp.float32
        )
        weights = jnp.exp(cosine_score_matrix).astype(jnp.bfloat16)
        softmax_denominators = jnp.sum(weights.astype(jnp.float32), axis=1)
        softmax_scaled_captions = jnp.dot(weights, text_block, preferred_element_type=jnp.float32)
        global_rows = row_map(jnp.arange(block_rows, dtype=jnp.int32))
        onehot = (pair_index[:, None] == global_rows[None, :]).astype(jnp.bfloat16)
        diagonal_matched_scores = jnp.dot(onehot, text_block, preferred_element_type=jnp.float32)
        return (softmax_denominators, softmax_scaled_captions, diagonal_matched_scores)

    return fold_texts


def on_device(
    images, conv_kernels, norm_gains, expand_weight, project_weight, head_weight, texts, pair_index
):
    phase_pick = lax.axis_index("phase")
    kernel = conv_kernels[0]
    gain_vec = norm_gains[0]
    expand = expand_weight[0]
    project_out = project_weight[0]
    first_out, front_one, mlp_one = section_forward(images, kernel, gain_vec, expand, project_out)
    handed = hand_over(first_out)
    second_out, front_two, mlp_two = section_forward(handed, kernel, gain_vec, expand, project_out)
    embed, head_back = jax.vjp(
        lambda inner: head_part(inner, head_weight), second_out.astype(jnp.float32)
    )
    vector_lowered_total = embed.astype(jnp.bfloat16)
    caption_unit_vectors = unit_text(texts)
    image_rows = embed.shape[0]
    embed_width = embed.shape[1]
    text_rows = caption_unit_vectors.shape[0]
    share_count = 1
    share_rows = text_rows // share_count

    def share_map(rows_now):
        return rows_now // share_rows * text_rows + rows_now % share_rows

    start_state = (
        jnp.zeros((image_rows,), jnp.float32),
        jnp.zeros((image_rows, embed_width), jnp.float32),
        jnp.zeros((image_rows, embed_width), jnp.float32),
    )
    fold_texts = make_fold(vector_lowered_total, pair_index, share_map)
    softmax_denominators, softmax_scaled_captions, diagonal_matched_scores = fold_texts(
        start_state, lax.all_gather(caption_unit_vectors, "batch", axis=0, tiled=True), jnp.int32(0)
    )
    encoder_output_slope = inverse_softness_factor * (
        softmax_scaled_captions / softmax_denominators[:, None] - diagonal_matched_scores
    )
    (grad_second,) = head_back(encoder_output_slope)
    grad_first_in = section_backward(grad_second, front_two, mlp_two)
    returned = hand_over(grad_first_in.astype(jnp.bfloat16))
    grad_images = section_backward(returned.astype(jnp.float32), front_one, mlp_one)
    chosen = jnp.where(phase_pick == 0, grad_images, grad_first_in)
    return chosen[None]


def solution(mesh):
    return jax.shard_map(
        on_device,
        mesh=mesh,
        in_specs=(
            P("batch", None, None, None),
            P("phase", None, None, None),
            P("phase", None),
            P("phase", None, "mp"),
            P("phase", "mp", None),
            P(),
            P("batch", None),
            P("batch"),
        ),
        out_specs=P("phase", "batch", None, None, None),
        check_vma=False,
    )
```

profile of v0, /device:TPU:0, one launch (start us, length us, event | category | flops | bytes accessed | tf_op | source)
XLA Modules:
  0.0 215.0 jit_solution(14726889605407176546)
XLA Ops:
  6.5 1.1 copy.165
  7.6 1.0 reshape.232
  8.6 1.9 copy.122
  10.5 1.7 gather_fusion
  12.2 5.0 %copy.121 = f32[16,16,768]{1,0,2:T(8,128)} copy(f32[16,16,768]{2,1,0:T(8,128)S(1)} %bitcast.116) | data formatting | bytes 1572864 | tf_op jit(solution)/shard_map/jvp()/gather | solution.py:27
  17.2 9.9 %bitcast_reduce_fusion.1 = (f32[8,16]{1,0:T(8,128)S(1)}, f32[768,16,8]{1,2,0:T(8,128)}) fusion(f32[16,16,768]{1,0,2:T(8,128)} %copy.121, bf16[8,16,768]{1,0,2:T(8,128)(2,1)} %copy.122), kind=kOutput, calls=%fused_computation.161 | convolution fusion | flops 18972544 | bytes 1376768 | tf_op jit(solution)/shard_map/jvp(oic,bic->boc)/dot_general | solution.py:29
  27.1 2.3 %copy.123 = f32[768,16,8]{0,1,2:T(8,128)S(1)} copy(f32[768,16,8]{1,2,0:T(8,128)} %get-tuple-element.18) | data formatting | bytes 786432 | tf_op jit(solution)/shard_map/jvp(oic,bic->boc)/dot_general | solution.py:29
  29.4 0.2 multiply_reduce_fusion.3
  29.7 0.1 multiply_convert_fusion.3
  29.8 1.5 multiply_convert_fusion.1
  31.3 0.1 dot_general.57
  31.4 3.0 %fusion.16 = bf16[8,4,4,768]{3,0,2,1:T(8,128)(2,1)} fusion(bf16[1,1536,768]{2,1,0:T(8,128)(2,1)} %param.22, bf16[8,4,4,1536]{3,2,1,0:T(4,128)(2,1)S(1)} %dot_general.57), kind=kOutput, calls=%fused_computation.21 | convolution fusion | flops 302088192 | bytes 2949120 | tf_op jit(solution)/shard_map/jvp()/dot_general | solution.py:48
  34.4 0.2 all-reduce.7.cloned.1.call-start
  34.7 0.1 fusion.93
  34.8 25.0 %all-reduce.5.cloned.1.call-done = bf16[8,4,4,768]{3,0,2,1:T(8,128)(2,1)} async-done(((bf16[8,4,4,768]{3,0,2,1:T(8,128)(2,1)}), bf16[8,4,4,768]{3,0,2,1:T(8,128)(2,1)}) %all-reduce.5.cloned.1.call-update) | async-done | bytes 196624 | tf_op jit(solution)/shard_map/psum | solution.py:66
  59.8 1.0 add_convert_fusion.1
  60.9 1.4 collective-permute-done
  62.3 1.9 copy.127
  64.2 9.9 %bitcast_reduce_fusion = (f32[8,16]{1,0:T(8,128)S(1)}, f32[768,8,16]{2,1,0:T(8,128)}) fusion(bf16[8,16,768]{1,0,2:T(8,128)(2,1)} %copy.127, f32[16,16,768]{1,0,2:T(8,128)} %copy.121), kind=kOutput, calls=%fused_computation.160 | convolution fusion | flops 18972544 | bytes 1376768 | tf_op jit(solution)/shard_map/jvp(oic,bic->boc)/dot_general | solution.py:29
  74.0 2.3 %copy.129 = f32[768,8,16]{0,2,1:T(8,128)S(1)} copy(f32[768,8,16]{2,1,0:T(8,128)} %get-tuple-element.22) | data formatting | bytes 786432 | tf_op jit(solution)/shard_map/jvp(oic,bic->boc)/dot_general | solution.py:29
  76.4 0.2 multiply_reduce_fusion.2
  76.6 0.1 multiply_convert_fusion.2
  76.7 1.5 multiply_convert_fusion
  78.2 0.1 dot_general.61
  78.3 3.0 %fusion.19 = bf16[8,4,4,768]{3,0,2,1:T(8,128)(2,1)} fusion(bf16[1,1536,768]{2,1,0:T(8,128)(2,1)} %param.22, bf16[8,4,4,1536]{3,2,1,0:T(4,128)(2,1)S(1)} %dot_general.61), kind=kOutput, calls=%fused_computation.22 | convolution fusion | flops 302088192 | bytes 2949120 | tf_op jit(solution)/shard_map/jvp()/dot_general | solution.py:48
  81.3 0.1 fusion.94
  81.4 30.6 %all_gather.3 = bf16[64,1024]{1,0:T(8,128)(2,1)S(1)} all-gather(bf16[8,1024]{1,0:T(8,128)(2,1)S(1)} %fusion.94), channel_id=1, replica_groups=mesh['batch'=8,'phase'=2,'mp'=2] {'batch'}, dimensions={0}, use_global_device_ids=true | all-gather | bytes 147456 | tf_op jit(solution)/shard_map/all_gather | solution.py:137
  112.0 1.1 convert_reduce_fusion
  113.1 0.1 multiply_reduce_fusion.8
  113.2 0.2 multiply_reduce_fusion.7
  113.4 1.9 multiply_reduce_fusion.5
  115.3 0.3 convert_reduce_fusion.1
  115.7 0.1 convolution_divide_fusion
  115.8 0.3 multiply_reduce_fusion.4
  116.1 0.6 multiply_reduce_fusion.6
  116.8 0.2 fusion.125
  117.0 0.1 add_multiply_fusion
  117.2 3.6 %fusion.22 = bf16[128,768]{1,0:T(8,128)(2,1)S(1)} fusion(bf16[1,768,1536]{2,1,0:T(8,128)(2,1)S(1)} %copy-done, f32[128,1536]{1,0:T(8,128)} %get-tuple-element.24, bf16[128,768]{1,0:T(8,128)(2,1)S(1)} %reshape.234, bf16[1,1536,768]{2,1,0:T(8,128)(2,1)} %param.22), kind=kOutput, calls=%fused_computation.23 | convolution fusion | flops 608108544 | bytes 5898240 | tf_op jit(solution)/shard_map/transpose(jvp())/dot_general | solution.py:45
  120.8 0.7 copy.134
  121.6 0.3 all-reduce.11.cloned.1.call-start
  121.9 2.4 %copy.136 = f32[8,16,768]{2,0,1:T(8,128)S(1)} copy(f32[8,16,768]{1,0,2:T(8,128)} %bitcast.109) | data formatting | bytes 786432 | tf_op jit(solution)/shard_map/jvp(oic,bic->boc)/transpose | solution.py:29
  124.3 0.1 copy.135
  124.4 19.8 %all-reduce.9.cloned.1.call-done = bf16[8,4,4,768]{3,0,2,1:T(8,128)(2,1)} async-done(((bf16[8,4,4,768]{3,0,2,1:T(8,128)(2,1)}), bf16[8,4,4,768]{3,0,2,1:T(8,128)(2,1)}) %all-reduce.9.cloned.1.call-update) | async-done | bytes 196624 | tf_op jit(solution)/shard_map/psum | solution.py:66
  144.1 1.1 multiply_reduce_fusion.1
  145.3 1.2 fusion.91
  146.4 1.1 broadcast_add_fusion.1
  147.5 2.2 %copy.138 = f32[768,8,16]{2,1,0:T(8,128)} copy(f32[768,8,16]{0,1,2:T(8,128)S(1)} %bitcast.118) | data formatting | bytes 786432 | tf_op jit(solution)/shard_map/transpose(jvp(oic,bic->boc))/transpose | solution.py:29
  149.7 9.1 %convolution_bitcast_fusion.1 = f32[8,16,768]{1,0,2:T(8,128)} fusion(f32[768,8,16]{2,1,0:T(8,128)} %copy.138, f32[16,16,768]{1,0,2:T(8,128)} %copy.121), kind=kOutput, calls=%fused_computation.20 | convolution fusion | flops 18874368 | bytes 1572864 | tf_op jit(solution)/shard_map/transpose(jvp(oic,bic->boc))/dot_general | solution.py:29
  158.7 2.4 %copy.140 = f32[8,16,768]{2,0,1:T(8,128)S(1)} copy(f32[8,16,768]{1,0,2:T(8,128)} %convolution_bitcast_fusion.1) | data formatting | bytes 786432 | tf_op jit(solution)/shard_map/transpose(jvp(oic,bic->boc))/transpose | solution.py:29
  161.2 1.4 collective-permute-done.1
  162.7 0.7 copy-done.3
  163.3 0.1 copy.141
  163.5 3.5 %fusion.25 = bf16[128,768]{1,0:T(8,128)(2,1)S(1)} fusion(bf16[1,768,1536]{2,1,0:T(8,128)(2,1)S(1)} %copy-done, f32[128,1536]{1,0:T(8,128)} %get-tuple-element.20, bf16[128,768]{1,0:T(8,128)(2,1)S(1)} %reshape.238, bf16[1,1536,768]{2,1,0:T(8,128)(2,1)} %param.22), kind=kOutput, calls=%fused_computation.24 | convolution fusion | flops 608206848 | bytes 5898240 | tf_op jit(solution)/shard_map/transpose(jvp())/dot_general | solution.py:45
  167.1 0.7 copy.142
  167.9 2.4 %copy.144 = f32[8,16,768]{2,0,1:T(8,128)S(1)} copy(f32[8,16,768]{1,0,2:T(8,128)} %bitcast.108) | data formatting | bytes 786432 | tf_op jit(solution)/shard_map/jvp(oic,bic->boc)/transpose | solution.py:29
  170.3 0.1 copy.143
  170.4 20.0 %all-reduce.11.cloned.1.call-done = bf16[8,4,4,768]{3,0,2,1:T(8,128)(2,1)} async-done(((bf16[8,4,4,768]{3,0,2,1:T(8,128)(2,1)}), bf16[8,4,4,768]{3,0,2,1:T(8,128)(2,1)}) %all-reduce.11.cloned.1.call-update) | async-done | bytes 196624 | tf_op jit(solution)/shard_map/psum | solution.py:66
  190.4 1.1 multiply_reduce_fusion
  191.5 1.2 fusion.92
  192.7 1.1 broadcast_add_fusion
  193.8 2.3 %copy.146 = f32[768,8,16]{2,1,0:T(8,128)} copy(f32[768,8,16]{0,1,2:T(8,128)S(1)} %bitcast.117) | data formatting | bytes 786432 | tf_op jit(solution)/shard_map/transpose(jvp(oic,bic->boc))/transpose | solution.py:29
  196.1 9.1 %convolution_bitcast_fusion = f32[8,16,768]{1,0,2:T(8,128)} fusion(f32[768,8,16]{2,1,0:T(8,128)} %copy.146, f32[16,16,768]{1,0,2:T(8,128)} %copy.121), kind=kOutput, calls=%fused_computation.19 | convolution fusion | flops 18874368 | bytes 1572864 | tf_op jit(solution)/shard_map/transpose(jvp(oic,bic->boc))/dot_general | solution.py:29
  205.1 2.4 %copy.148 = f32[8,16,768]{2,0,1:T(8,128)S(1)} copy(f32[8,16,768]{1,0,2:T(8,128)} %convolution_bitcast_fusion) | data formatting | bytes 786432 | tf_op jit(solution)/shard_map/transpose(jvp(oic,bic->boc))/transpose | solution.py:29
  207.6 0.9 copy.149
  (56 shorter events, 0.9 us)
Async XLA Ops:
  6.5 23.3 %copy-start = (bf16[1,768,1536]{2,1,0:T(8,128)(2,1)S(1)}, bf16[1,768,1536]{2,1,0:T(8,128)(2,1)}, u32[]{:S(2)}) copy-start(bf16[1,768,1536]{2,1,0:T(8,128)(2,1)} %param.21) | copy-start | bytes 7077892
  6.5 3.9 %copy-start.1 = (s32[256]{0:T(256)S(1)}, s32[256]{0:T(256)}, u32[]{:S(2)}) copy-start(s32[256]{0:T(256)} %constant.120) | copy-start | bytes 3076
  6.5 53.2 %all-reduce.5.cloned.1.call-start = ((), (), s32[]{:S(2)}) async-start(), calls=%async_computation | async-start | bytes 393216 | tf_op jit(solution)/shard_map/psum | solution.py:66
  27.1 2.5 %copy-start.9 = (f32[1,768]{1,0:T(1,128)S(1)}, f32[1,768]{1,0:T(1,128)}, u32[]{:S(2)}) copy-start(f32[1,768]{1,0:T(1,128)} %param.20) | copy-start | bytes 9220
  31.4 3.3 %copy-start.8 = (bf16[8,1024]{1,0:T(8,128)(2,1)S(1)}, bf16[8,1024]{1,0:T(8,128)(2,1)}, u32[]{:S(2)}) copy-start(bf16[8,1024]{1,0:T(8,128)(2,1)} %param.24) | copy-start | bytes 49156
  31.4 28.4 %copy-start.5 = (bf16[8,4,4,768]{3,2,1,0:T(4,128)(2,1)S(1)}, bf16[8,4,4,768]{3,2,1,0:T(4,128)(2,1)}, u32[]{:S(2)}) copy-start(bf16[8,4,4,768]{3,2,1,0:T(4,128)(2,1)} %param.18) | copy-start | bytes 589828
  34.4 77.6 %all-reduce.7.cloned.1.call-start = ((), (), s32[]{:S(2)}) async-start(), calls=%async_computation.1 | async-start | bytes 393216 | tf_op jit(solution)/shard_map/psum | solution.py:66
  60.8 1.5 collective-permute-start
  81.3 34.5 %copy-start.10 = (s32[8]{0:T(128)S(1)}, s32[8]{0:T(128)}, u32[]{:S(2)}) copy-start(s32[8]{0:T(128)} %param.25) | copy-start | bytes 100
  81.3 62.8 %all-reduce.9.cloned.1.call-start = ((), (), s32[]{:S(2)}) async-start(), calls=%async_computation.2 | async-start | bytes 393216 | tf_op jit(solution)/shard_map/psum | solution.py:66
  112.0 4.1 %copy-start.2 = (bf16[768,1024]{1,0:T(8,128)(2,1)S(1)}, bf16[768,1024]{1,0:T(8,128)(2,1)}, u32[]{:S(2)}) copy-start(bf16[768,1024]{1,0:T(8,128)(2,1)} %param.23) | copy-start | bytes 4718596
  117.1 44.0 %copy-start.6 = (f32[8,768]{1,0:T(8,128)}, f32[8,768]{1,0:T(8,128)S(1)}, u32[]{:S(2)}) copy-start(f32[8,768]{1,0:T(8,128)S(1)} %add_multiply_fusion) | copy-start | bytes 73732
  121.6 68.8 %all-reduce.11.cloned.1.call-start = ((), (), s32[]{:S(2)}) async-start(), calls=%async_computation.3 | async-start | bytes 393216 | tf_op jit(solution)/shard_map/psum | solution.py:66
  161.1 1.5 collective-permute-start.1
  162.7 0.7 copy-start.3
  205.1 2.4 %copy-start.4 = (bf16[8,4,4,768]{3,0,2,1:T(8,128)(2,1)S(1)}, bf16[8,4,4,768]{3,0,2,1:T(8,128)(2,1)}, u32[]{:S(2)}) copy-start(bf16[8,4,4,768]{3,0,2,1:T(8,128)(2,1)} %copy-done.3) | copy-start | bytes 589828
  205.1 2.4 %copy-start.7 = (f32[8,768]{1,0:T(8,128)S(1)}, f32[8,768]{1,0:T(8,128)}, u32[]{:S(2)}) copy-start(f32[8,768]{1,0:T(8,128)} %copy-done.6) | copy-start | bytes 73732
Sparse Core Ops, SparseCore 0:
  34.5 25.1 all-reduce.4
  81.4 22.3 all-reduce.6
  121.7 22.3 all-reduce.8
  168.0 22.3 all-reduce.10
where the time goes:
time: 216 us; the launch traced here: 215 us
  waiting for transfers between devices  67.7 us (31%)
  matrix products  57.2 us (26%)
  local copies, waits for them, and re-layouts  34.9 us (16%)
  blocking collectives  30.6 us (14%)
  between operations  13.5 us (6%)
  other arithmetic  10.5 us (5%)
    psum x4, waiting for transfers between devices, hidden_total(): return lax.psum(values.astype(jnp.bfloat16), 'mp').astype(jnp.float32)  64.8 us
    dot_general x4, matrix products, depthwise(): jnp.einsum('oic,bic->boc', operator, flat, precision=lax.Precision.HIGHEST)  37.9 us
    all_gather x1, blocking collectives, on_device(): lax.all_gather(caption_unit_vectors, 'batch', axis=0, tiled=True)  30.6 us
    transpose x6, local copies, waits for them, and re-layouts, depthwise(): jnp.einsum('oic,bic->boc', operator, flat, precision=lax.Precision.HIGHEST)  13.9 us
    dot_general x4, matrix products, mlp_part(): jnp.dot(flattened, expand, preferred_element_type=jnp.float32)  10.1 us
    gather x2, local copies, waits for them, and re-layouts, depthwise(): kernel[tap_row, tap_col]  6.7 us
    dot_general x2, matrix products, mlp_part(): jnp.dot(hidden, project_out, preferred_element_type=jnp.float32)  5.97 us
    reshape x3, local copies, waits for them, and re-layouts, depthwise(): values.reshape(values.shape[0], grid_side * grid_side, values.shape[3])  4.71 us
  transfers between devices with their start and end apart: 6, of which 5 were waited for; matrix products, arithmetic and copies ran while one was open for 2% of the time, Pallas kernels for 0%

commit v1 on v0

--- a/solution.py
+++ b/solution.py
@@ -63,7 +63,7 @@
 
 
 def hidden_total(values):
-    return lax.psum(values.astype(jnp.bfloat16), "mp").astype(jnp.float32)
+    return jnp.sum(lax.all_gather(values.astype(jnp.bfloat16), "mp"), axis=0).astype(jnp.float32)
 
 
 def hand_over(values):

time: 216 us -> 162 us (0.75)
  waiting for transfers between devices: 67.7 us -> 1.42 us
  blocking collectives: 30.6 us -> 60.4 us
  between operations: 13.5 us -> 0.47 us
  local copies, waits for them, and re-layouts: 34.9 us -> 32.1 us
    psum x4 -> x0, waiting for transfers between devices: 64.8 us -> none  [hidden_total(): return lax.psum(values.astype(jnp.bfloat16), 'mp').astype(jnp.float32)]
    all_gather x0 -> x4, blocking collectives: none -> 29.1 us  [hidden_total(): lax.all_gather(values.astype(jnp.bfloat16), 'mp')]
    transpose x6 -> x4, local copies, waits for them, and re-layouts: 13.9 us -> 9.25 us  [depthwise(): jnp.einsum('oic,bic->boc', operator, flat, precision=lax.Precision.HIGHEST)]
    add_any x2 -> x0, other arithmetic: 2.17 us -> none  [normalize_last(): centred = values - jnp.mean(values, axis=-1, keepdims=True)]
  transfers between devices with their start and end apart: 6 -> 2, of which waited for: 5 -> 1; matrix products, arithmetic and copies ran while one was open for 2% -> 0% of each run, Pallas kernels for 0% -> 0%
where the time goes in v1:
time: 162 us; the launch traced here: 161 us
  blocking collectives  60.4 us (37%)
  matrix products  56.3 us (35%)
  local copies, waits for them, and re-layouts  32.1 us (20%)
  other arithmetic  10.3 us (6%)
    dot_general x4, matrix products, depthwise(): jnp.einsum('oic,bic->boc', operator, flat, precision=lax.Precision.HIGHEST)  38 us
    all_gather x1, blocking collectives, on_device(): lax.all_gather(caption_unit_vectors, 'batch', axis=0, tiled=True)  31.3 us
    all_gather x4, blocking collectives, hidden_total(): lax.all_gather(values.astype(jnp.bfloat16), 'mp')  29.1 us
    dot_general x4, matrix products, mlp_part(): jnp.dot(flattened, expand, preferred_element_type=jnp.float32)  11.6 us
    transpose x4, local copies, waits for them, and re-layouts, depthwise(): jnp.einsum('oic,bic->boc', operator, flat, precision=lax.Precision.HIGHEST)  9.25 us
    gather x2, local copies, waits for them, and re-layouts, depthwise(): kernel[tap_row, tap_col]  6.84 us
    dot_general x2, matrix products, mlp_part(): jnp.dot(hidden, project_out, preferred_element_type=jnp.float32)  4.84 us
    dot_general x2, local copies, waits for them, and re-layouts, depthwise(): jnp.einsum('oic,bic->boc', operator, flat, precision=lax.Precision.HIGHEST)  4.64 us
  transfers between devices with their start and end apart: 2, of which 1 were waited for; matrix products, arithmetic and copies ran while one was open for 0% of the time, Pallas kernels for 0%

profile of v1, /device:TPU:0, one launch (start us, length us, event | category | flops | bytes accessed | tf_op | source)
XLA Modules:
  0.0 161.1 jit_solution(7638159513696866442)
XLA Ops:
  0.0 1.1 copy.142
  1.1 1.8 %gather_fusion = f32[256,768]{1,0:T(8,128)S(1)} fusion(f32[7,7,768]{2,1,0:T(8,128)S(1)} %bitcast.117, s32[256]{0:T(256)} %constant.125), kind=kCustom, calls=%fused_computation | custom fusion | bytes 1574912 | tf_op jit(solution)/shard_map/jvp()/gather | solution.py:27
  3.0 5.0 %copy.88 = f32[16,16,768]{1,0,2:T(8,128)} copy(f32[16,16,768]{2,1,0:T(8,128)S(1)} %bitcast.120) | data formatting | bytes 1572864 | tf_op jit(solution)/shard_map/jvp()/gather | solution.py:27
  8.0 1.9 %copy.89 = bf16[8,16,768]{1,0,2:T(8,128)(2,1)} copy(bf16[8,16,768]{2,1,0:T(8,128)(2,1)S(1)} %reshape.268) | data formatting | bytes 393216 | tf_op jit(solution)/shard_map/jvp()/reshape | solution.py:28
  9.9 9.9 %fusion.126 = f32[768,16,8]{1,2,0:T(8,128)} fusion(f32[16,16,768]{1,0,2:T(8,128)} %copy.88, bf16[8,16,768]{1,0,2:T(8,128)(2,1)} %copy.89), kind=kOutput, calls=%fused_computation.180 | convolution fusion | flops 18874368 | bytes 1376256 | tf_op jit(solution)/shard_map/jvp(oic,bic->boc)/dot_general | solution.py:29
  19.8 2.3 %copy.90 = f32[768,16,8]{0,1,2:T(8,128)S(1)} copy(f32[768,16,8]{1,2,0:T(8,128)} %fusion.126) | data formatting | bytes 786432 | tf_op jit(solution)/shard_map/jvp(oic,bic->boc)/dot_general | solution.py:29
  22.1 0.1 bitcast_reduce_fusion.3
  22.2 0.2 multiply_reduce_fusion.3
  22.5 0.1 multiply_convert_fusion.3
  22.6 1.5 multiply_convert_fusion.1
  24.1 0.1 dot_general.57
  24.2 2.3 %fusion.16 = bf16[8,4,4,768]{3,0,2,1:T(8,128)(2,1)S(1)} fusion(bf16[1,1536,768]{2,1,0:T(8,128)(2,1)} %param.22, bf16[8,4,4,1536]{3,2,1,0:T(4,128)(2,1)S(1)} %dot_general.57), kind=kOutput, calls=%fused_computation.21 | convolution fusion | flops 302088192 | bytes 2949120 | tf_op jit(solution)/shard_map/jvp()/dot_general | solution.py:48
  26.6 8.6 %all-gather = bf16[16,4,4,768]{3,0,2,1:T(8,128)(2,1)S(1)} all-gather(bf16[8,4,4,768]{3,0,2,1:T(8,128)(2,1)S(1)} %fusion.16), channel_id=2, replica_groups=mesh['batch'=8,'phase'=2,'mp'=2] {'mp'}, dimensions={0}, use_global_device_ids=true | all-gather | bytes 589824 | tf_op jit(solution)/shard_map/all_gather | solution.py:66
  35.2 0.1 add_convert_fusion.1
  35.4 0.1 fusion.91
  35.6 31.3 %all_gather.27 = bf16[64,1024]{1,0:T(8,128)(2,1)S(1)} all-gather(bf16[8,1024]{1,0:T(8,128)(2,1)S(1)} %fusion.92), channel_id=1, replica_groups=mesh['batch'=8,'phase'=2,'mp'=2] {'batch'}, dimensions={0}, use_global_device_ids=true | all-gather | bytes 147456 | tf_op jit(solution)/shard_map/all_gather | solution.py:137
  66.9 0.6 fusion.109
  67.4 1.9 %copy.92 = bf16[8,16,768]{1,0,2:T(8,128)(2,1)} copy(bf16[8,16,768]{2,0,1:T(8,128)(2,1)S(1)} %bitcast.122) | data formatting | bytes 393216 | tf_op jit(solution)/shard_map/jvp()/reshape | solution.py:28
  69.4 10.0 %fusion.127 = f32[768,8,16]{2,1,0:T(8,128)} fusion(bf16[8,16,768]{1,0,2:T(8,128)(2,1)} %copy.92, f32[16,16,768]{1,0,2:T(8,128)} %copy.88), kind=kOutput, calls=%fused_computation.181 | convolution fusion | flops 18874368 | bytes 1376256 | tf_op jit(solution)/shard_map/jvp(oic,bic->boc)/dot_general | solution.py:29
  79.3 2.3 %copy.94 = f32[768,8,16]{0,2,1:T(8,128)S(1)} copy(f32[768,8,16]{2,1,0:T(8,128)} %fusion.127) | data formatting | bytes 786432 | tf_op jit(solution)/shard_map/jvp(oic,bic->boc)/dot_general | solution.py:29
  81.6 0.1 bitcast_reduce_fusion.1
  81.8 0.2 multiply_reduce_fusion.2
  82.0 0.1 multiply_convert_fusion.2
  82.1 1.6 multiply_convert_fusion
  83.7 1.8 %dot_general.61 = bf16[8,4,4,1536]{3,2,1,0:T(4,128)(2,1)} reshape(bf16[128,1536]{1,0:T(8,128)(2,1)} %get-tuple-element.11) | data formatting | bytes 786432 | tf_op jit(solution)/shard_map/jvp()/dot_general | solution.py:48
  85.5 2.5 %fusion.19 = bf16[8,4,4,768]{3,0,2,1:T(8,128)(2,1)S(1)} fusion(bf16[1,1536,768]{2,1,0:T(8,128)(2,1)} %param.22, bf16[8,4,4,1536]{3,2,1,0:T(4,128)(2,1)} %dot_general.61), kind=kOutput, calls=%fused_computation.22 | convolution fusion | flops 302088192 | bytes 2949120 | tf_op jit(solution)/shard_map/jvp()/dot_general | solution.py:48
  88.1 6.3 %all-gather.1 = bf16[16,4,4,768]{3,0,2,1:T(8,128)(2,1)S(1)} all-gather(bf16[8,4,4,768]{3,0,2,1:T(8,128)(2,1)S(1)} %fusion.19), channel_id=3, replica_groups=mesh['batch'=8,'phase'=2,'mp'=2] {'mp'}, dimensions={0}, use_global_device_ids=true | all-gather | bytes 589824 | tf_op jit(solution)/shard_map/all_gather | solution.py:66
  94.5 0.1 multiply_reduce_fusion.8
  94.7 0.2 multiply_reduce_fusion.7
  94.9 0.5 multiply_reduce_fusion.5
  95.3 0.3 convert_reduce_fusion.1
  95.7 0.1 convolution_divide_fusion
  95.8 0.3 multiply_reduce_fusion.4
  96.1 0.6 multiply_reduce_fusion.6
  96.8 0.2 fusion.125
  97.1 0.6 copy-done.6
  97.8 4.2 %fusion.22 = bf16[128,768]{1,0:T(8,128)(2,1)} fusion(bf16[1,768,1536]{2,1,0:T(8,128)(2,1)S(1)} %copy-done, f32[128,1536]{1,0:T(8,128)} %get-tuple-element.12, bf16[128,768]{1,0:T(8,128)(2,1)S(1)} %reshape.270, bf16[1,1536,768]{2,1,0:T(8,128)(2,1)} %param.22), kind=kOutput, calls=%fused_computation.23 | convolution fusion | flops 608108544 | bytes 5898240 | tf_op jit(solution)/shard_map/transpose(jvp())/dot_general | solution.py:45
  102.0 1.0 convert_element_type.170
  103.1 6.6 %all_gather.28 = bf16[2,8,4,4,768]{4,1,3,2,0:T(8,128)(2,1)S(1)} all-gather(bf16[1,8,4,4,768]{4,1,3,2,0:T(8,128)(2,1)S(1)} %copy.97), channel_id=1, replica_groups=mesh['batch'=8,'phase'=2,'mp'=2] {'mp'}, dimensions={0}, use_global_device_ids=true | all-gather | bytes 589824 | tf_op jit(solution)/shard_map/all_gather | solution.py:66
  109.7 0.8 reduce_sum.244
  110.4 1.0 convert.6
  111.4 0.2 multiply_reduce_fusion.1
  111.6 0.7 multiply_multiply_fusion.5
  112.3 1.0 fusion.95
  113.3 0.9 add_bitcast_fusion.1
  114.2 2.3 %copy.101 = f32[768,8,16]{2,1,0:T(8,128)} copy(f32[768,8,16]{0,2,1:T(8,128)S(1)} %add_bitcast_fusion.1) | data formatting | bytes 786432 | tf_op jit(solution)/shard_map/transpose(jvp(oic,bic->boc))/transpose | solution.py:29
  116.5 9.1 %convolution_bitcast_fusion.1 = f32[8,16,768]{1,0,2:T(8,128)} fusion(f32[768,8,16]{2,1,0:T(8,128)} %copy.101, f32[16,16,768]{1,0,2:T(8,128)} %copy.88), kind=kOutput, calls=%fused_computation.20 | convolution fusion | flops 18874368 | bytes 1572864 | tf_op jit(solution)/shard_map/transpose(jvp(oic,bic->boc))/dot_general | solution.py:29
  125.5 2.4 %copy.103 = f32[8,16,768]{2,0,1:T(8,128)S(1)} copy(f32[8,16,768]{1,0,2:T(8,128)} %convolution_bitcast_fusion.1) | data formatting | bytes 786432 | tf_op jit(solution)/shard_map/transpose(jvp(oic,bic->boc))/transpose | solution.py:29
  128.0 1.4 collective-permute-done.1
  129.5 0.1 copy.104
  129.5 0.7 reshape.272
  130.3 4.3 %fusion.25 = bf16[128,768]{1,0:T(8,128)(2,1)} fusion(bf16[1,768,1536]{2,1,0:T(8,128)(2,1)S(1)} %copy-done, f32[128,1536]{1,0:T(8,128)} %get-tuple-element.10, bf16[128,768]{1,0:T(8,128)(2,1)} %reshape.272, bf16[1,1536,768]{2,1,0:T(8,128)(2,1)} %param.22), kind=kOutput, calls=%fused_computation.24 | convolution fusion | flops 608206848 | bytes 5898240 | tf_op jit(solution)/shard_map/transpose(jvp())/dot_general | solution.py:45
  134.6 1.0 convert_element_type.178
  135.6 7.6 %all_gather.29 = bf16[2,8,4,4,768]{4,1,3,2,0:T(8,128)(2,1)S(1)} all-gather(bf16[1,8,4,4,768]{4,1,3,2,0:T(8,128)(2,1)S(1)} %copy.105), channel_id=1, replica_groups=mesh['batch'=8,'phase'=2,'mp'=2] {'mp'}, dimensions={0}, use_global_device_ids=true | all-gather | bytes 589824 | tf_op jit(solution)/shard_map/all_gather | solution.py:66
  143.2 0.8 reduce_sum.247
  144.0 1.0 convert.7
  145.0 0.2 multiply_reduce_fusion
  145.2 0.7 multiply_multiply_fusion.4
  145.9 0.3 fusion.96
  146.2 0.2 add_bitcast_fusion
  146.4 2.3 %copy.109 = f32[768,8,16]{2,1,0:T(8,128)} copy(f32[768,8,16]{0,2,1:T(8,128)S(1)} %add_bitcast_fusion) | data formatting | bytes 786432 | tf_op jit(solution)/shard_map/transpose(jvp(oic,bic->boc))/transpose | solution.py:29
  148.7 9.1 %convolution_bitcast_fusion = f32[8,16,768]{1,0,2:T(8,128)} fusion(f32[768,8,16]{2,1,0:T(8,128)} %copy.109, f32[16,16,768]{1,0,2:T(8,128)} %copy.88), kind=kOutput, calls=%fused_computation.19 | convolution fusion | flops 18874368 | bytes 1572864 | tf_op jit(solution)/shard_map/transpose(jvp(oic,bic->boc))/dot_general | solution.py:29
  157.7 2.4 %copy.111 = f32[8,16,768]{2,0,1:T(8,128)S(1)} copy(f32[8,16,768]{1,0,2:T(8,128)} %convolution_bitcast_fusion) | data formatting | bytes 786432 | tf_op jit(solution)/shard_map/transpose(jvp(oic,bic->boc))/transpose | solution.py:29
  160.2 0.9 copy.112
  (60 shorter events, 1.0 us)
Async XLA Ops:
  0.0 22.6 %copy-start = (bf16[1,768,1536]{2,1,0:T(8,128)(2,1)S(1)}, bf16[1,768,1536]{2,1,0:T(8,128)(2,1)}, u32[]{:S(2)}) copy-start(bf16[1,768,1536]{2,1,0:T(8,128)(2,1)} %param.21) | copy-start | bytes 7077892
  2.9 5.0 %copy-start.4 = (bf16[8,4,4,768]{3,2,1,0:T(4,128)(2,1)S(1)}, bf16[8,4,4,768]{3,2,1,0:T(4,128)(2,1)}, u32[]{:S(2)}) copy-start(bf16[8,4,4,768]{3,2,1,0:T(4,128)(2,1)} %param.18) | copy-start | bytes 589828
  19.8 2.7 %copy-start.13 = (f32[1,768]{1,0:T(1,128)S(1)}, f32[1,768]{1,0:T(1,128)}, u32[]{:S(2)}) copy-start(f32[1,768]{1,0:T(1,128)} %param.20) | copy-start | bytes 9220
  22.4 1.8 %copy-start.11 = (f32[8,16]{1,0:T(8,128)}, f32[8,16]{1,0:T(8,128)S(1)}, u32[]{:S(2)}) copy-start(f32[8,16]{1,0:T(8,128)S(1)} %multiply_reduce_fusion.3) | copy-start | bytes 1540
  24.2 11.0 %copy-start.5 = (bf16[8,4,4,768]{3,2,1,0:T(4,128)(2,1)S(1)}, bf16[8,4,4,768]{3,2,1,0:T(4,128)(2,1)}, u32[]{:S(2)}) copy-start(bf16[8,4,4,768]{3,2,1,0:T(4,128)(2,1)} %param.18) | copy-start | bytes 589828
  24.2 11.1 %copy-start.10 = (bf16[8,1024]{1,0:T(8,128)(2,1)S(1)}, bf16[8,1024]{1,0:T(8,128)(2,1)}, u32[]{:S(2)}) copy-start(bf16[8,1024]{1,0:T(8,128)(2,1)} %param.24) | copy-start | bytes 49156
  35.3 32.2 %collective-permute-start = (bf16[8,4,4,768]{3,0,2,1:T(8,128)(2,1)S(1)}, bf16[8,4,4,768]{3,0,2,1:T(8,128)(2,1)S(1)}, u32[]{:S(2)}, u32[]{:S(2)}) collective-permute-start(bf16[8,4,4,768]{3,0,2,1:T(8,128)(2,1)S(1)} %add_convert_fusion.1), channel_id=1, source_target_pairs={{0,2},{2,0},{1,3},{3,1},{4,6},{6,4},{5,7},{7,5},{8,10},{10,8},{9,1... | collective-permute-start | bytes 589832 | tf_op jit(solution)/shard_map/ppermute | solution.py:11
  81.9 3.6 %copy-start.12 = (f32[8,16]{1,0:T(8,128)}, f32[8,16]{1,0:T(8,128)S(1)}, u32[]{:S(2)}) copy-start(f32[8,16]{1,0:T(8,128)S(1)} %multiply_reduce_fusion.2) | copy-start | bytes 1540
  82.0 3.6 %copy-start.9 = (f32[8,16]{1,0:T(8,128)}, f32[8,16]{1,0:T(8,128)S(1)}, u32[]{:S(2)}) copy-start(f32[8,16]{1,0:T(8,128)S(1)} %fusion.106) | copy-start | bytes 1540
  85.5 9.3 %copy-start.1 = (bf16[768,1024]{1,0:T(8,128)(2,1)S(1)}, bf16[768,1024]{1,0:T(8,128)(2,1)}, u32[]{:S(2)}) copy-start(bf16[768,1024]{1,0:T(8,128)(2,1)} %param.23) | copy-start | bytes 4718596
  88.1 7.8 %copy-start.14 = (s32[8]{0:T(128)S(1)}, s32[8]{0:T(128)}, u32[]{:S(2)}) copy-start(s32[8]{0:T(128)} %param.25) | copy-start | bytes 100
  88.1 7.7 %copy-start.15 = (s32[64]{0:T(128)S(1)}, s32[64]{0:T(128)}, u32[]{:S(2)}) copy-start(s32[64]{0:T(128)} %fusion.109) | copy-start | bytes 772
  97.1 0.6 copy-start.6
  125.5 2.4 %copy-start.7 = (f32[8,768]{1,0:T(8,128)S(1)}, f32[8,768]{1,0:T(8,128)}, u32[]{:S(2)}) copy-start(f32[8,768]{1,0:T(8,128)} %copy-done.6) | copy-start | bytes 73732
  128.0 1.5 collective-permute-start.1
  129.5 5.1 %copy-start.2 = (bf16[8,4,4,768]{3,0,2,1:T(8,128)(2,1)}, bf16[8,4,4,768]{3,0,2,1:T(8,128)(2,1)S(1)}, u32[]{:S(2)}) copy-start(bf16[8,4,4,768]{3,0,2,1:T(8,128)(2,1)S(1)} %collective-permute-done.1) | copy-start | bytes 589828
  157.7 2.4 %copy-start.3 = (bf16[8,4,4,768]{3,0,2,1:T(8,128)(2,1)S(1)}, bf16[8,4,4,768]{3,0,2,1:T(8,128)(2,1)}, u32[]{:S(2)}) copy-start(bf16[8,4,4,768]{3,0,2,1:T(8,128)(2,1)} %copy-done.2) | copy-start | bytes 589828
  157.7 2.4 %copy-start.8 = (f32[8,768]{1,0:T(8,128)S(1)}, f32[8,768]{1,0:T(8,128)}, u32[]{:S(2)}) copy-start(f32[8,768]{1,0:T(8,128)} %copy-done.6) | copy-start | bytes 73732
